TPU v7x, 128 devices: a whole 4x4x4 slice. The times are simulated.
128 devices in a mesh: dp: 8 (over x, core), eig: 16 (over y, z).
Axes of the slice: x: 4, y: 4, z: 4, core: 2. Of those that a mesh axis runs over, the one named last changes fastest.
Arguments:
- acts: bfloat16 [4096, 8192], P(('dp', 'eig')), may hold values from -6 to 6
- grads: bfloat16 [4096, 8192], P(('dp', 'eig')), may hold values from -6 to 6
- act_basis: bfloat16 [4096, 8192], P('eig'), may hold values from -0.0625 to 0.0625
- grad_basis: bfloat16 [4096, 8192], P('eig'), may hold values from -0.0625 to 0.0625
- eigenvalues: float32 [4096, 4096], P('eig'), may hold values from 0.05 to 20
- query_grads: bfloat16 [32, 256, 4096], P('dp', None, 'eig'), may hold values from -6 to 6
- query_acts: bfloat16 [32, 256, 4096], P('dp'), may hold values from -6 to 6
- cand_local: int32 [8, 16], P('dp'), may hold values from 0 to 7, as said below
- seq_lengths: int32 [8, 8], P('dp'), may hold values from 1 to 128, 512 in all within a row
Outputs:
- scores: float32 [32, 16], P('dp')
Inputs may be any that keep to these rules, and one draw needn't show every extreme that they name: `cand_local`: entry j of an owner's list names a sequence of dp shard j // 2; the 2 entries of one list that name one shard differ. `seq_lengths`: row d lists the lengths of the 8 sequences packed in order in dp shard d's 512 token rows; they sum to 512.
All inputs are finite; a program needn't handle non-finite values.
Results may differ from a plain program's by a relative error of at most 0.006.
Values may be sent and summed in bfloat16 or wider, within the bound.
No kernel may reach another device: no remote copies, remote signals or barrier semaphores. Data moves between devices by JAX's collectives and lax.ppermute only.
A program may use at most 128 MiB of HBM per device.

v0:
```python
import math
import jax
import jax.numpy as jnp
from jax import lax
from jax.sharding import PartitionSpec as P

DAMPING = 0.1


def shards(
    acts,
    grads,
    act_basis,
    grad_basis,
    eigenvalues,
    query_grads,
    query_acts,
    cand_local,
    seq_lengths,
):
    block_width = act_basis.shape[0]
    queries = query_grads.shape[0]
    full_width = query_acts.shape[2]
    seq_count = seq_lengths.shape[1]
    group_rows = acts.shape[0] * lax.axis_size("eig")
    max_len = 2 * group_rows // seq_count
    pick_lists = lax.all_to_all(cand_local, "dp", split_axis=1, concat_axis=0, tiled=True)
    owners = pick_lists.shape[0]
    per_shard = pick_lists.shape[1]
    lengths = seq_lengths[0]
    offsets = jnp.cumsum(lengths) - lengths
    chosen = (
        pick_lists[:, :, None] == jnp.arange(seq_count, dtype=jnp.int32)[None, None, :]
    ).astype(jnp.int32)
    pick_len = jnp.sum(chosen * lengths[None, None, :], axis=2)
    pick_start = jnp.sum(chosen * offsets[None, None, :], axis=2)
    within = jnp.arange(max_len, dtype=jnp.int32)
    is_live = within[None, None, :] < pick_len[:, :, None]
    row_index = jnp.where(is_live, pick_start[:, :, None] + within[None, None, :], -1).reshape(-1)
    select = (row_index[:, None] == jnp.arange(group_rows, dtype=jnp.int32)[None, :]).astype(
        jnp.bfloat16
    )

    def rotate_and_pack(rows, basis):
        shard_rows = lax.all_gather(rows, "eig", axis=0, tiled=True)
        rotated = jnp.dot(shard_rows, basis.T, preferred_element_type=jnp.float32).astype(
            jnp.bfloat16
        )
        rotated = lax.optimization_barrier(rotated)
        packed = jnp.dot(select, rotated, preferred_element_type=jnp.float32).astype(jnp.bfloat16)
        packed = packed.reshape(owners, per_shard * max_len, block_width)
        return lax.all_to_all(packed, "dp", split_axis=0, concat_axis=0, tiled=True)

    act_narrow = rotate_and_pack(acts, act_basis)
    act_recv = lax.all_gather(act_narrow, "eig", axis=2, tiled=True)
    grad_recv = rotate_and_pack(grads, grad_basis)
    slot_count = owners * per_shard * max_len
    grad_flat = grad_recv.reshape(slot_count, block_width).astype(jnp.float32)
    act_flat = act_recv.reshape(slot_count, full_width)
    damped = eigenvalues + DAMPING
    query_outer = jnp.einsum(
        "qti,qtk->qik", query_grads, query_acts, preferred_element_type=jnp.float32
    )
    precond = (query_outer / damped[None]).astype(jnp.bfloat16)
    precond = lax.optimization_barrier(precond.reshape(queries * block_width, full_width))
    projected = lax.dot_general(
        act_flat, precond, (((1,), (1,)), ((), ())), preferred_element_type=jnp.float32
    )
    projected = lax.optimization_barrier(projected).reshape(slot_count, queries, block_width)
    per_token = jnp.sum(projected * grad_flat[:, None, :], axis=2)
    partial_sums = jnp.sum(per_token.reshape(owners * per_shard, max_len, queries), axis=1).T
    summed = lax.psum(partial_sums, "eig")
    score_scale = 1.0 / (full_width * 4.0 * math.sqrt(query_acts.shape[1]))
    return summed * score_scale


def solution(mesh):
    placed = (
        P(("dp", "eig"), None),
        P(("dp", "eig"), None),
        P("eig", None),
        P("eig", None),
        P("eig", None),
        P("dp", None, "eig"),
        P("dp", None, None),
        P("dp", None),
        P("dp", None),
    )
    return jax.shard_map(
        shards, mesh=mesh, in_specs=placed, out_specs=P("dp", None), check_vma=False
    )
```

profile of v0, /device:TPU:0, one launch (start us, length us, event | category | flops | bytes accessed | tf_op | source)
XLA Modules:
  0.0 363.8 jit_solution(16105542730583716110)
XLA Ops:
  6.5 0.7 all-gather.4.cloned.1.call-update
  7.3 0.7 all-gather.8.cloned.1.call-update
  8.0 0.5 broadcast.27
  8.5 1.3 reduce.3
  9.8 0.7 all_to_all.16
  10.5 4.4 %all-to-all-start = ((s32[1,8,2]{2,0,1:T(1,128)}), s32[1,8,2]{2,0,1:T(1,128)S(1)}, u32[]{:S(2)}, u32[]{:S(2)}) async-start(s32[1,8,2]{2,0,1:T(1,128)} %bitcast), calls=%async_computation | async-start | bytes 8192 | tf_op jit(solution)/shard_map/all_to_all | solution.py:27
  15.0 0.8 reduce-window.8
  15.8 0.7 bitcast_subtract_fusion
  16.5 3.7 %all-to-all-done = s32[1,8,2]{2,0,1:T(1,128)S(1)} async-done(((s32[1,8,2]{2,0,1:T(1,128)}), s32[1,8,2]{2,0,1:T(1,128)S(1)}, u32[]{:S(2)}, u32[]{:S(2)}) %all-to-all-start) | async-done | bytes 96 | tf_op jit(solution)/shard_map/all_to_all | solution.py:27
  20.3 0.9 select_reduce_fusion.1
  21.2 0.1 copy.27
  21.3 0.1 compare_select_fusion
  21.4 61.6 %all-gather.4.cloned.1.call-done = bf16[512,8192]{1,0:T(8,128)(2,1)} async-done(((bf16[32,8192]{1,0:T(8,128)(2,1)}), bf16[512,8192]{1,0:T(8,128)(2,1)}) %all-gather.4.cloned.1.call-update) | async-done | bytes 8388624 | tf_op jit(solution)/shard_map/all_gather | solution.py:45
  83.0 6.9 %convolution_convert_fusion.1 = bf16[512,256]{1,0:T(8,128)(2,1)S(1)} fusion(bf16[512,8192]{1,0:T(8,128)(2,1)} %all-gather.4.cloned.1.call-done, bf16[256,8192]{1,0:T(8,128)(2,1)} %param.11), kind=kOutput, calls=%fused_computation.11 | convolution fusion | flops 2147614720 | bytes 12845056 | tf_op jit(solution)/shard_map/dot_general | solution.py:46
  89.9 1.1 fusion.2
  91.0 20.1 %all_to_all.23 = bf16[8,256,256]{2,1,0:T(8,128)(2,1)} all-to-all(bf16[8,256,256]{2,1,0:T(8,128)(2,1)S(1)} %bitcast.28), channel_id=1, replica_groups=mesh['dp'=8,'eig'=16] {'dp'}, dimensions={0} | all-to-all | bytes 2097152 | tf_op jit(solution)/shard_map/all_to_all | solution.py:52
  111.2 4.8 %broadcast_add_fusion = f32[256,4096]{1,0:T(8,128)} fusion(f32[256,4096]{1,0:T(8,128)} %param.13), kind=kLoop, calls=%fused_computation.7 | loop fusion | flops 1048576 | bytes 8388608 | tf_op jit(solution)/shard_map/add | solution.py:60
  115.9 39.8 %all-gather.8.cloned.1.call-done = bf16[512,8192]{1,0:T(8,128)(2,1)} async-done(((bf16[32,8192]{1,0:T(8,128)(2,1)}), bf16[512,8192]{1,0:T(8,128)(2,1)}) %all-gather.8.cloned.1.call-update) | async-done | bytes 8388624 | tf_op jit(solution)/shard_map/all_gather | solution.py:45
  155.7 6.9 %convolution_convert_fusion = bf16[512,256]{1,0:T(8,128)(2,1)S(1)} fusion(bf16[512,8192]{1,0:T(8,128)(2,1)} %all-gather.8.cloned.1.call-done, bf16[256,8192]{1,0:T(8,128)(2,1)} %param.12), kind=kOutput, calls=%fused_computation.10 | convolution fusion | flops 2147614720 | bytes 12845056 | tf_op jit(solution)/shard_map/dot_general | solution.py:46
  162.6 1.9 fusion.3
  164.5 4.3 %all-to-all-start.2 = ((bf16[8,256,256]{2,1,0:T(8,128)(2,1)}), bf16[8,256,256]{2,1,0:T(8,128)(2,1)S(1)}, u32[]{:S(2)}, u32[]{:S(2)}) async-start(bf16[8,256,256]{2,1,0:T(8,128)(2,1)} %bitcast.9), calls=%async_computation.2 | async-start | bytes 2097152 | tf_op jit(solution)/shard_map/all_to_all | solution.py:52
  168.7 9.2 %divide_convert_fusion = bf16[4,256,4096]{2,1,0:T(8,128)(2,1)} fusion(f32[256,4096]{1,0:T(8,128)} %broadcast_add_fusion, bf16[4,256,256]{2,1,0:T(8,128)(2,1)S(1)} %copy-done, bf16[4,256,4096]{2,1,0:T(8,128)(2,1)} %param.15), kind=kOutput, calls=%fused_computation | convolution fusion | flops 2155872256 | bytes 21495808 | tf_op jit(solution)/shard_map/qti,qtk->qik/dot_general | solution.py:61
  177.9 6.7 %all-to-all-done.2 = bf16[8,256,256]{2,1,0:T(8,128)(2,1)S(1)} async-done(((bf16[8,256,256]{2,1,0:T(8,128)(2,1)}), bf16[8,256,256]{2,1,0:T(8,128)(2,1)S(1)}, u32[]{:S(2)}, u32[]{:S(2)}) %all-to-all-start.2) | async-done | bytes 1048608 | tf_op jit(solution)/shard_map/all_to_all | solution.py:52
  184.7 1.1 copy-done.2
  185.7 1.4 convert.1
  187.1 90.2 %all-gather.6.cloned.1.call-done = bf16[8,256,4096]{2,1,0:T(8,128)(2,1)} async-done(((bf16[8,256,256]{2,1,0:T(8,128)(2,1)}), bf16[8,256,4096]{2,1,0:T(8,128)(2,1)}) %all-gather.6.cloned.1.call-update) | async-done | bytes 16777232 | tf_op jit(solution)/shard_map/all_gather | solution.py:55
  277.4 24.1 %fusion.6 = f32[2048,1024]{1,0:T(8,128)} fusion(bf16[2048,4096]{1,0:T(8,128)(2,1)} %bitcast.35, bf16[1024,4096]{1,0:T(8,128)(2,1)} %bitcast.36), kind=kOutput, calls=%fused_computation.19 | convolution fusion | flops 17179869184 | bytes 33554432 | tf_op jit(solution)/shard_map/dot_general | solution.py:66
  301.5 10.6 %reshape.106 = f32[2048,4,256]{2,1,0:T(4,128)} reshape(f32[2048,1024]{1,0:T(8,128)} %fusion.6) | data formatting | bytes 16777216 | tf_op jit(solution)/shard_map/reshape | solution.py:69
  312.1 6.3 %multiply_reduce_fusion = f32[2048,4]{1,0:T(8,128)S(1)} fusion(f32[2048,4,256]{2,1,0:T(4,128)} %reshape.106, f32[2048,256]{1,0:T(8,128)S(1)} %convert.1), kind=kLoop, calls=%fused_computation.1 | loop fusion | flops 4186112 | bytes 10518528 | tf_op jit(solution)/shard_map/reduce_sum | solution.py:70
  318.4 0.1 bitcast_reduce_fusion
  318.6 38.1 %psum.7 = f32[4,16]{1,0:T(4,128)S(1)} all-reduce(f32[4,16]{1,0:T(4,128)S(1)} %bitcast.29), channel_id=1, replica_groups=mesh['dp'=8,'eig'=16] {'eig'}, use_global_device_ids=true, to_apply=%region_5.6 | all-reduce | flops 64 | bytes 512 | tf_op jit(solution)/shard_map/psum | solution.py:72
  356.7 0.6 broadcast_multiply_fusion
  (12 shorter events, 0.3 us)
Async XLA Ops:
  6.5 162.2 %copy-start = (bf16[4,256,256]{2,1,0:T(8,128)(2,1)S(1)}, bf16[4,256,256]{2,1,0:T(8,128)(2,1)}, u32[]{:S(2)}) copy-start(bf16[4,256,256]{2,1,0:T(8,128)(2,1)} %param.14) | copy-start | bytes 1572868
  6.5 76.4 %all-gather.4.cloned.1.call-start = ((), (), s32[]{:S(2)}) async-start(), calls=%async_computation.3 | async-start | bytes 8912896 | tf_op jit(solution)/shard_map/all_gather | solution.py:45
  7.3 148.4 %all-gather.8.cloned.1.call-start = ((), (), s32[]{:S(2)}) async-start(), calls=%async_computation.5 | async-start | bytes 8912896 | tf_op jit(solution)/shard_map/all_gather | solution.py:45
  10.5 9.7 %all-to-all-start = ((s32[1,8,2]{2,0,1:T(1,128)}), s32[1,8,2]{2,0,1:T(1,128)S(1)}, u32[]{:S(2)}, u32[]{:S(2)}) async-start(s32[1,8,2]{2,0,1:T(1,128)} %bitcast), calls=%async_computation | async-start | bytes 8192 | tf_op jit(solution)/shard_map/all_to_all | solution.py:27
  14.9 262.5 %all-gather.6.cloned.1.call-start = ((), (), s32[]{:S(2)}) async-start(), calls=%async_computation.4 | async-start | bytes 17825792 | tf_op jit(solution)/shard_map/all_gather | solution.py:55
  164.5 20.2 %all-to-all-start.2 = ((bf16[8,256,256]{2,1,0:T(8,128)(2,1)}), bf16[8,256,256]{2,1,0:T(8,128)(2,1)S(1)}, u32[]{:S(2)}, u32[]{:S(2)}) async-start(bf16[8,256,256]{2,1,0:T(8,128)(2,1)} %bitcast.9), calls=%async_computation.2 | async-start | bytes 2097152 | tf_op jit(solution)/shard_map/all_to_all | solution.py:52
  184.7 1.1 copy-start.2
  301.5 55.8 %copy-start.1 = (bf16[4,256,256]{2,1,0:T(8,128)(2,1)S(1)}, bf16[4,256,256]{2,1,0:T(8,128)(2,1)}, u32[]{:S(2)}) copy-start(bf16[4,256,256]{2,1,0:T(8,128)(2,1)} %param.14) | copy-start | bytes 1572868
Sparse Core Ops, SparseCore 0:
  9.5 73.4 all-gather.3
  85.1 70.4 all-gather.7
  157.8 119.5 all-gather.5
where the time goes:
time: 364 us
  waiting for transfers between devices  203 us (56%)
  blocking collectives  58.3 us (16%)
  matrix products  50.1 us (14%)
  other arithmetic  16.9 us (5%)
  local copies, waits for them, and re-layouts  13.2 us (4%)
  between operations  13.2 us (4%)
  starting transfers between devices  8.75 us (2%)
    all_gather x2, waiting for transfers between devices, rotate_and_pack(): shard_rows = lax.all_gather(rows, 'eig', axis=0, tiled=True)  101 us
    all_gather x1, waiting for transfers between devices, shards(): act_recv = lax.all_gather(act_narrow, 'eig', axis=2, tiled=True)  90.2 us
    psum x1, blocking collectives, shards(): summed = lax.psum(partial_sums, 'eig')  38.1 us
    dot_general x1, matrix products, shards(): lax.dot_general(act_flat, precond, (((1,), (1,)), ((), ())), preferred_el...  24.1 us
    all_to_all x1, blocking collectives, rotate_and_pack(): return lax.all_to_all(packed, 'dp', split_axis=0, concat_axis=0, tiled=True)  20.1 us
    dot_general x2, matrix products, rotate_and_pack(): jnp.dot(shard_rows, basis.T, preferred_element_type=jnp.float32)  13.9 us
    reshape x1, local copies, waits for them, and re-layouts, shards(): lax.optimization_barrier(projected)  10.6 us
    dot_general x1, matrix products, shards(): jnp.einsum('qti,qtk->qik', query_grads, query_acts, preferred_element_typ...  9.21 us
  transfers between devices with their start and end apart: 5, of which 5 were waited for; matrix products, arithmetic and copies ran while one was open for 10% of the time, Pallas kernels for 0%

commit v1 on v0

--- a/solution.py
+++ b/solution.py
@@ -69,7 +69,7 @@
     projected = lax.optimization_barrier(projected).reshape(slot_count, queries, block_width)
     per_token = jnp.sum(projected * grad_flat[:, None, :], axis=2)
     partial_sums = jnp.sum(per_token.reshape(owners * per_shard, max_len, queries), axis=1).T
-    summed = lax.psum(partial_sums, "eig")
+    summed = lax.all_gather(partial_sums, "eig").sum(axis=0)
     score_scale = 1.0 / (full_width * 4.0 * math.sqrt(query_acts.shape[1]))
     return summed * score_scale
 

time: 364 us -> 349 us (0.959)
  blocking collectives: 58.3 us -> 42.9 us
    psum x1 -> x0, blocking collectives: 38.1 us -> none  [shards(): summed = lax.psum(partial_sums, 'eig')]
    all_gather x0 -> x1, blocking collectives: none -> 22.7 us  [shards(): summed = lax.all_gather(partial_sums, 'eig').sum(axis=0)]
  transfers between devices with their start and end apart: 5 -> 5, of which waited for: 5 -> 5; matrix products, arithmetic and copies ran while one was open for 10% -> 11% of each run, Pallas kernels for 0% -> 0%
where the time goes in v1:
time: 349 us; the launch traced here: 348 us
  waiting for transfers between devices  203 us (58%)
  matrix products  50.1 us (14%)
  blocking collectives  42.9 us (12%)
  other arithmetic  16.9 us (5%)
  local copies, waits for them, and re-layouts  13.2 us (4%)
  between operations  13.2 us (4%)
  starting transfers between devices  8.75 us (3%)
    all_gather x2, waiting for transfers between devices, rotate_and_pack(): shard_rows = lax.all_gather(rows, 'eig', axis=0, tiled=True)  101 us
    all_gather x1, waiting for transfers between devices, shards(): act_recv = lax.all_gather(act_narrow, 'eig', axis=2, tiled=True)  90.2 us
    dot_general x1, matrix products, shards(): lax.dot_general(act_flat, precond, (((1,), (1,)), ((), ())), preferred_el...  24.1 us
    all_gather x1, blocking collectives, shards(): summed = lax.all_gather(partial_sums, 'eig').sum(axis=0)  22.7 us
    all_to_all x1, blocking collectives, rotate_and_pack(): return lax.all_to_all(packed, 'dp', split_axis=0, concat_axis=0, tiled=True)  20.1 us
    dot_general x2, matrix products, rotate_and_pack(): jnp.dot(shard_rows, basis.T, preferred_element_type=jnp.float32)  13.9 us
    reshape x1, local copies, waits for them, and re-layouts, shards(): lax.optimization_barrier(projected)  10.6 us
    dot_general x1, matrix products, shards(): jnp.einsum('qti,qtk->qik', query_grads, query_acts, preferred_element_typ...  9.21 us
  transfers between devices with their start and end apart: 5, of which 5 were waited for; matrix products, arithmetic and copies ran while one was open for 11% of the time, Pallas kernels for 0%

profile of v1, /device:TPU:0, one launch (start us, length us, event | category | flops | bytes accessed | tf_op | source)
XLA Modules:
  0.0 348.4 jit_solution(9284170612990531727)
XLA Ops:
  6.5 0.7 all-gather.6.cloned.1.call-update
  7.3 0.7 all-gather.10.cloned.1.call-update
  8.0 0.5 broadcast.27
  8.5 1.3 reduce.4
  9.8 0.7 all_to_all.16
  10.5 4.4 %all-to-all-start = ((s32[1,8,2]{2,0,1:T(1,128)}), s32[1,8,2]{2,0,1:T(1,128)S(1)}, u32[]{:S(2)}, u32[]{:S(2)}) async-start(s32[1,8,2]{2,0,1:T(1,128)} %bitcast), calls=%async_computation | async-start | bytes 8192 | tf_op jit(solution)/shard_map/all_to_all | solution.py:27
  15.0 0.8 reduce-window.8
  15.8 0.7 bitcast_subtract_fusion
  16.5 3.7 %all-to-all-done = s32[1,8,2]{2,0,1:T(1,128)S(1)} async-done(((s32[1,8,2]{2,0,1:T(1,128)}), s32[1,8,2]{2,0,1:T(1,128)S(1)}, u32[]{:S(2)}, u32[]{:S(2)}) %all-to-all-start) | async-done | bytes 96 | tf_op jit(solution)/shard_map/all_to_all | solution.py:27
  20.3 0.9 select_reduce_fusion.1
  21.2 0.1 copy.27
  21.3 0.1 compare_select_fusion
  21.4 61.6 %all-gather.6.cloned.1.call-done = bf16[512,8192]{1,0:T(8,128)(2,1)} async-done(((bf16[32,8192]{1,0:T(8,128)(2,1)}), bf16[512,8192]{1,0:T(8,128)(2,1)}) %all-gather.6.cloned.1.call-update) | async-done | bytes 8388624 | tf_op jit(solution)/shard_map/all_gather | solution.py:45
  83.0 6.9 %convolution_convert_fusion.1 = bf16[512,256]{1,0:T(8,128)(2,1)S(1)} fusion(bf16[512,8192]{1,0:T(8,128)(2,1)} %all-gather.6.cloned.1.call-done, bf16[256,8192]{1,0:T(8,128)(2,1)} %param.11), kind=kOutput, calls=%fused_computation.11 | convolution fusion | flops 2147614720 | bytes 12845056 | tf_op jit(solution)/shard_map/dot_general | solution.py:46
  89.9 1.1 fusion.2
  91.0 20.1 %all_to_all.23 = bf16[8,256,256]{2,1,0:T(8,128)(2,1)} all-to-all(bf16[8,256,256]{2,1,0:T(8,128)(2,1)S(1)} %bitcast.30), channel_id=1, replica_groups=mesh['dp'=8,'eig'=16] {'dp'}, dimensions={0} | all-to-all | bytes 2097152 | tf_op jit(solution)/shard_map/all_to_all | solution.py:52
  111.2 4.8 %broadcast_add_fusion = f32[256,4096]{1,0:T(8,128)} fusion(f32[256,4096]{1,0:T(8,128)} %param.13), kind=kLoop, calls=%fused_computation.7 | loop fusion | flops 1048576 | bytes 8388608 | tf_op jit(solution)/shard_map/add | solution.py:60
  115.9 39.8 %all-gather.10.cloned.1.call-done = bf16[512,8192]{1,0:T(8,128)(2,1)} async-done(((bf16[32,8192]{1,0:T(8,128)(2,1)}), bf16[512,8192]{1,0:T(8,128)(2,1)}) %all-gather.10.cloned.1.call-update) | async-done | bytes 8388624 | tf_op jit(solution)/shard_map/all_gather | solution.py:45
  155.7 6.9 %convolution_convert_fusion = bf16[512,256]{1,0:T(8,128)(2,1)S(1)} fusion(bf16[512,8192]{1,0:T(8,128)(2,1)} %all-gather.10.cloned.1.call-done, bf16[256,8192]{1,0:T(8,128)(2,1)} %param.12), kind=kOutput, calls=%fused_computation.10 | convolution fusion | flops 2147614720 | bytes 12845056 | tf_op jit(solution)/shard_map/dot_general | solution.py:46
  162.6 1.9 fusion.3
  164.5 4.3 %all-to-all-start.2 = ((bf16[8,256,256]{2,1,0:T(8,128)(2,1)}), bf16[8,256,256]{2,1,0:T(8,128)(2,1)S(1)}, u32[]{:S(2)}, u32[]{:S(2)}) async-start(bf16[8,256,256]{2,1,0:T(8,128)(2,1)} %bitcast.9), calls=%async_computation.2 | async-start | bytes 2097152 | tf_op jit(solution)/shard_map/all_to_all | solution.py:52
  168.7 9.2 %divide_convert_fusion = bf16[4,256,4096]{2,1,0:T(8,128)(2,1)} fusion(f32[256,4096]{1,0:T(8,128)} %broadcast_add_fusion, bf16[4,256,256]{2,1,0:T(8,128)(2,1)S(1)} %copy-done, bf16[4,256,4096]{2,1,0:T(8,128)(2,1)} %param.15), kind=kOutput, calls=%fused_computation | convolution fusion | flops 2155872256 | bytes 21495808 | tf_op jit(solution)/shard_map/qti,qtk->qik/dot_general | solution.py:61
  177.9 6.7 %all-to-all-done.2 = bf16[8,256,256]{2,1,0:T(8,128)(2,1)S(1)} async-done(((bf16[8,256,256]{2,1,0:T(8,128)(2,1)}), bf16[8,256,256]{2,1,0:T(8,128)(2,1)S(1)}, u32[]{:S(2)}, u32[]{:S(2)}) %all-to-all-start.2) | async-done | bytes 1048608 | tf_op jit(solution)/shard_map/all_to_all | solution.py:52
  184.7 1.1 copy-done.2
  185.7 1.4 convert.1
  187.1 90.2 %all-gather.8.cloned.1.call-done = bf16[8,256,4096]{2,1,0:T(8,128)(2,1)} async-done(((bf16[8,256,256]{2,1,0:T(8,128)(2,1)}), bf16[8,256,4096]{2,1,0:T(8,128)(2,1)}) %all-gather.8.cloned.1.call-update) | async-done | bytes 16777232 | tf_op jit(solution)/shard_map/all_gather | solution.py:55
  277.4 24.1 %fusion.6 = f32[2048,1024]{1,0:T(8,128)} fusion(bf16[2048,4096]{1,0:T(8,128)(2,1)} %bitcast.37, bf16[1024,4096]{1,0:T(8,128)(2,1)} %bitcast.38), kind=kOutput, calls=%fused_computation.19 | convolution fusion | flops 17179869184 | bytes 33554432 | tf_op jit(solution)/shard_map/dot_general | solution.py:66
  301.5 10.6 %reshape.106 = f32[2048,4,256]{2,1,0:T(4,128)} reshape(f32[2048,1024]{1,0:T(8,128)} %fusion.6) | data formatting | bytes 16777216 | tf_op jit(solution)/shard_map/reshape | solution.py:69
  312.1 6.3 %multiply_reduce_fusion = f32[2048,4]{1,0:T(8,128)S(1)} fusion(f32[2048,4,256]{2,1,0:T(4,128)} %reshape.106, f32[2048,256]{1,0:T(8,128)S(1)} %convert.1), kind=kLoop, calls=%fused_computation.1 | loop fusion | flops 4186112 | bytes 10518528 | tf_op jit(solution)/shard_map/reduce_sum | solution.py:70
  318.4 0.1 bitcast_reduce_fusion
  318.6 22.7 %all-gather.1 = f32[16,4,16]{2,1,0:T(4,128)S(1)} all-gather(f32[1,4,16]{2,1,0:T(4,128)S(1)} %bitcast.31), channel_id=2, replica_groups=mesh['dp'=8,'eig'=16] {'eig'}, dimensions={0}, use_global_device_ids=true | all-gather | bytes 4352 | tf_op jit(solution)/shard_map/all_gather | solution.py:72
  341.3 0.6 broadcast_multiply_fusion
  (13 shorter events, 0.4 us)
Async XLA Ops:
  6.5 162.2 %copy-start = (bf16[4,256,256]{2,1,0:T(8,128)(2,1)S(1)}, bf16[4,256,256]{2,1,0:T(8,128)(2,1)}, u32[]{:S(2)}) copy-start(bf16[4,256,256]{2,1,0:T(8,128)(2,1)} %param.14) | copy-start | bytes 1572868
  6.5 76.4 %all-gather.6.cloned.1.call-start = ((), (), s32[]{:S(2)}) async-start(), calls=%async_computation.3 | async-start | bytes 8912896 | tf_op jit(solution)/shard_map/all_gather | solution.py:45
  7.3 148.4 %all-gather.10.cloned.1.call-start = ((), (), s32[]{:S(2)}) async-start(), calls=%async_computation.5 | async-start | bytes 8912896 | tf_op jit(solution)/shard_map/all_gather | solution.py:45
  10.5 9.7 %all-to-all-start = ((s32[1,8,2]{2,0,1:T(1,128)}), s32[1,8,2]{2,0,1:T(1,128)S(1)}, u32[]{:S(2)}, u32[]{:S(2)}) async-start(s32[1,8,2]{2,0,1:T(1,128)} %bitcast), calls=%async_computation | async-start | bytes 8192 | tf_op jit(solution)/shard_map/all_to_all | solution.py:27
  14.9 262.5 %all-gather.8.cloned.1.call-start = ((), (), s32[]{:S(2)}) async-start(), calls=%async_computation.4 | async-start | bytes 17825792 | tf_op jit(solution)/shard_map/all_gather | solution.py:55
  164.5 20.2 %all-to-all-start.2 = ((bf16[8,256,256]{2,1,0:T(8,128)(2,1)}), bf16[8,256,256]{2,1,0:T(8,128)(2,1)S(1)}, u32[]{:S(2)}, u32[]{:S(2)}) async-start(bf16[8,256,256]{2,1,0:T(8,128)(2,1)} %bitcast.9), calls=%async_computation.2 | async-start | bytes 2097152 | tf_op jit(solution)/shard_map/all_to_all | solution.py:52
  184.7 1.1 copy-start.2
  301.5 40.4 %copy-start.1 = (bf16[4,256,256]{2,1,0:T(8,128)(2,1)S(1)}, bf16[4,256,256]{2,1,0:T(8,128)(2,1)}, u32[]{:S(2)}) copy-start(bf16[4,256,256]{2,1,0:T(8,128)(2,1)} %param.14) | copy-start | bytes 1572868
Sparse Core Ops, SparseCore 0:
  9.5 73.4 all-gather.5
  85.1 70.4 all-gather.9
  157.8 119.5 all-gather.7
